TPU v7x, 32 devices: a whole 2x2x4 slice. The times are simulated.
32 devices in a mesh: energy: 4 (over z), atom: 8 (over y, x, core).
Axes of the slice: x: 2, y: 2, z: 4, core: 2. Of those that a mesh axis runs over, the one named last changes fastest.
Arguments:
- t_mats: bfloat16 [4, 16, 2048], P('energy', 'atom'), may hold values from -0.75 to 0.75
- struct_table: bfloat16 [4, 64, 2048], P('energy'), may hold values from -0.359375 to 0.359375
- zone_atoms: int32 [16, 64], P('atom'), may hold values from 0 to 15, as said below
- zone_size: int32 [16], P('atom'), may hold values from 32 to 64
- pair_index: int32 [16, 384], P('atom'), may hold values from 0 to 63
- zone_link: int32 [16, 384], P('atom'), may hold values from 0 to 63
- weights: float32 [4, 2], P('energy'), may hold values from -1 to 1
Outputs:
- green: float32 [16, 2048], P('atom')
Inputs may be any that keep to these rules, and one draw needn't show every extreme that they name: Atom g is owned by index g // 2 of the atom axis; zone_atoms[g, 0] is g; the owner of every member of atom g's zone lies -4 to 3 steps from g's owner along the atom axis, counted around the axis, and both extreme offsets occur in every zone; members may repeat (periodic images).
All inputs are finite; a program needn't handle non-finite values.
Results may differ from a plain program's by a relative error of at most 0.003.
Values may be sent and summed in bfloat16 or wider, within the bound.
No kernel may reach another device: no remote copies, remote signals or barrier semaphores. Data moves between devices by JAX's collectives and lax.ppermute only.
A program may use at most 128 MiB of HBM per device.

v0:
```python
import jax
import jax.numpy as jnp
from jax import lax
from jax.sharding import PartitionSpec as P

L = 32
Z = 64
NB = 6


def real_form(block):
    parts = block.reshape(block.shape[:-1] + (2, L, L))
    real_part = parts[..., 0, :, :]
    imag_part = parts[..., 1, :, :]
    top_rows = jnp.concatenate([real_part, -imag_part], axis=-1)
    bottom_rows = jnp.concatenate([imag_part, real_part], axis=-1)
    return jnp.concatenate([top_rows, bottom_rows], axis=-2)


def take_rows(table, index):
    a_dev = index.shape[0]
    return jnp.take_along_axis(table, index.reshape(a_dev, -1), axis=1).reshape(index.shape)


def body(t_mats, struct_table, zone_atoms, zone_size, pair_index, zone_link, weights):
    e_dev, a_dev, block_flat = t_mats.shape
    window = lax.all_gather(t_mats, "atom", axis=1, tiled=True)
    coupling = jnp.arange(NB, dtype=jnp.int32)
    s2 = zone_link[:, :NB]
    s1 = take_rows(zone_link, s2[:, :, None] * NB + coupling)
    n1 = NB * NB
    slots = jnp.concatenate([s1.reshape(a_dev, n1), s2, jnp.zeros((a_dev, 1), jnp.int32)], axis=1)
    spots = slots[:, :, None] * NB + coupling
    pairs = take_rows(pair_index, spots)
    links = take_rows(zone_link, spots)
    members = take_rows(zone_atoms, slots)
    present = slots < zone_size[:, None]
    t_block = jnp.where(present[None, :, :, None], window[:, members], jnp.zeros((), jnp.bfloat16))
    t_real = real_form(t_block)
    g_real = real_form(struct_table[:, pairs])
    start_b = real_form(t_mats)[..., :L]
    start_f = start_b.astype(jnp.float32)
    is_zero = (slots == 0)[None, :, :, None, None]
    p1 = jnp.einsum(
        "easkij,eajc->easkic", g_real[:, :, :n1], start_b, preferred_element_type=jnp.float32
    )
    hit = (links[:, :n1] == 0)[None, :, :, :, None, None]
    coupled1 = jnp.sum(jnp.where(hit, p1, 0.0), axis=3).astype(jnp.bfloat16)
    col1 = jnp.einsum(
        "easij,easjc->easic", t_real[:, :, :n1], coupled1, preferred_element_type=jnp.float32
    ) + jnp.where(is_zero[:, :, :n1], start_f[:, :, None], 0.0)
    near2 = col1.astype(jnp.bfloat16).reshape(e_dev, a_dev, NB, NB, 2 * L, L)
    g2 = g_real[:, :, n1 : n1 + NB]
    coupled2 = jnp.einsum(
        "eamnij,eamnjc->eamic", g2, near2, preferred_element_type=jnp.float32
    ).astype(jnp.bfloat16)
    col2 = jnp.einsum(
        "eamij,eamjc->eamic",
        t_real[:, :, n1 : n1 + NB],
        coupled2,
        preferred_element_type=jnp.float32,
    ) + jnp.where(is_zero[:, :, n1 : n1 + NB], start_f[:, :, None], 0.0)
    near3 = col2.astype(jnp.bfloat16)
    coupled3 = jnp.einsum(
        "eanij,eanjc->eaic", g_real[:, :, n1 + NB], near3, preferred_element_type=jnp.float32
    ).astype(jnp.bfloat16)
    diagonal = (
        jnp.einsum(
            "eaij,eajc->eaic", t_real[:, :, n1 + NB], coupled3, preferred_element_type=jnp.float32
        )
        + start_f
    )
    real_rows = diagonal[:, :, :L, :].reshape(e_dev, a_dev, L * L)
    imag_rows = diagonal[:, :, L:, :].reshape(e_dev, a_dev, L * L)
    w_real = weights[:, 0][:, None, None]
    w_imag = weights[:, 1][:, None, None]
    green_real = jnp.sum(w_real * real_rows - w_imag * imag_rows, axis=0)
    green_imag = jnp.sum(w_real * imag_rows + w_imag * real_rows, axis=0)
    local_green = jnp.concatenate([green_real, green_imag], axis=-1)
    return lax.psum(local_green, "energy")


def solution(mesh):
    return jax.shard_map(
        body,
        mesh=mesh,
        in_specs=(
            P("energy", "atom", None),
            P("energy", None, None),
            P("atom", None),
            P("atom"),
            P("atom", None),
            P("atom", None),
            P("energy", None),
        ),
        out_specs=P("atom", None),
        check_vma=False,
    )
```

profile of v0, /device:TPU:0, one launch (start us, length us, event | category | flops | bytes accessed | tf_op | source)
XLA Modules:
  0.0 100.4 jit_solution(1606972806575443180)
XLA Ops:
  0.0 0.8 slice_bitcast_fusion.6
  0.8 0.1 add.205
  0.9 0.1 add.200
  1.0 0.1 reshape.652
  1.1 2.2 %gather_fusion.2 = s32[72]{0:T(128)S(1)} fusion(s32[2,384]{1,0:T(2,128)} %param.14, s32[72]{0:T(128)S(1)} %reshape.652), kind=kCustom, calls=%fused_computation.4 | custom fusion | bytes 1152 | tf_op jit(solution)/shard_map/jit(take_along_axis)/gather | solution.py:22
  3.3 0.1 reshape.655
  3.4 0.1 add.198
  3.7 0.1 add.215
  3.9 0.1 add.217
  4.1 9.7 %gather_fusion.4 = s32[516]{0:T(1024)S(1)} fusion(s32[2,384]{1,0:T(2,128)} %param.13, s32[516]{0:T(1024)S(1)} %reshape.682), kind=kCustom, calls=%fused_computation.clone | custom fusion | bytes 8256 | tf_op jit(solution)/shard_map/jit(take_along_axis)/gather | solution.py:22
  13.9 7.5 %gather_fusion.5 = s32[516]{0:T(1024)S(1)} fusion(s32[2,384]{1,0:T(2,128)S(1)} %copy-done.1, s32[516]{0:T(1024)S(1)} %reshape.682), kind=kCustom, calls=%fused_computation.1.clone | custom fusion | bytes 8256 | tf_op jit(solution)/shard_map/jit(take_along_axis)/gather | solution.py:22
  21.6 0.1 reshape.614
  21.7 0.1 reshape.608
  21.8 0.1 reshape.646
  22.0 3.4 %gather_fusion.1 = bf16[516,2048]{1,0:T(8,128)(2,1)S(1)} fusion(bf16[64,2048]{1,0:T(8,128)(2,1)S(1)} %bitcast.108, s32[1024]{0:T(1024)S(1)} %pad_clamp_fusion), kind=kCustom, calls=%fused_computation.3 | custom fusion | bytes 4229136 | tf_op jit(solution)/shard_map/gather | solution.py:40
  25.4 9.3 %reshape.609 = bf16[1,2,43,6,2,32,32]{6,5,4,3,2,1,0:T(8,128)(2,1)} reshape(bf16[516,2048]{1,0:T(8,128)(2,1)S(1)} %gather_fusion.1) | data formatting | bytes 4227072 | tf_op jit(solution)/shard_map/reshape | solution.py:12
  34.7 7.3 %slice_bitcast_fusion = (bf16[1,2,43,6,32,32]{5,4,3,2,1,0:T(8,128)(2,1)}, bf16[1,2,43,6,32,32]{5,4,3,2,1,0:T(8,128)(2,1)}) fusion(bf16[1,2,43,6,2,32,32]{6,5,4,3,2,1,0:T(8,128)(2,1)} %reshape.609), kind=kLoop, calls=%fused_computation.14 | loop fusion | bytes 4227072 | tf_op jit(solution)/shard_map/squeeze | solution.py:14
  42.1 1.5 %copy-done.3 = bf16[1,2,43,6,2,32,32]{6,5,4,3,2,1,0:T(8,128)(2,1)S(1)} copy-done((bf16[1,2,43,6,2,32,32]{6,5,4,3,2,1,0:T(8,128)(2,1)S(1)}, bf16[1,2,43,6,2,32,32]{6,5,4,3,2,1,0:T(8,128)(2,1)}, u32[]{:S(2)}) %copy-start.3) | copy-done | bytes 2113560
  43.6 2.5 %fusion.70 = bf16[1,2,43,6,32,32]{5,4,3,2,1,0:T(8,128)(2,1)} fusion(bf16[1,2,43,6,2,32,32]{6,5,4,3,2,1,0:T(8,128)(2,1)S(1)} %copy-done.3), kind=kLoop, calls=%fused_computation.115 | loop fusion | flops 528384 | bytes 2113536 | tf_op jit(solution)/shard_map/neg | solution.py:15
  46.1 0.1 reshape.616
  46.2 0.1 copy.45
  46.3 0.1 copy.44
  46.4 0.1 convert_bitcast_fusion
  46.5 9.5 %select_reduce_fusion = bf16[2,36,64,32]{2,3,1,0:T(8,128)(2,1)S(1)} fusion(pred[2,36,6]{2,1,0:T(8,128)(4,1)S(1)} %slice_compare_fusion, bf16[1,2,43,6,32,32]{5,4,3,2,1,0:T(8,128)(2,1)} %get-tuple-element.13, bf16[1,2,43,6,32,32]{5,4,3,2,1,0:T(8,128)(2,1)} %get-tuple-element.12, bf16[1,2,43,6,32,32]{5,4,3,2,1,0:T(8,128)(2,1)} %fusion.70, ...), kind=kOutput, calls=%fused_computation.13 | convolution fusion | flops 129024000 | bytes 3473840 | tf_op jit(solution)/shard_map/easkij,eajc->easkic/dot_general | solution.py:44
  56.0 0.1 shift-left_or_fusion
  56.1 0.1 reshape.658
  56.2 2.0 %gather_fusion.3 = s32[86]{0:T(128)S(1)} fusion(s32[2,64]{1,0:T(2,128)S(1)} %copy-done.2, s32[86]{0:T(128)S(1)} %reshape.658), kind=kCustom, calls=%fused_computation.5 | custom fusion | bytes 1376 | tf_op jit(solution)/shard_map/jit(take_along_axis)/gather | solution.py:22
  58.2 0.1 gather.23
  58.3 0.1 reshape.636
  58.4 10.7 %all_gather.3 = bf16[1,16,2048]{2,0,1:T(2,128)(2,1)S(1)} all-gather(bf16[1,2,2048]{2,0,1:T(2,128)(2,1)S(1)} %copy.27), channel_id=1, replica_groups=mesh['energy'=4,'atom'=8] {'atom'}, dimensions={1}, use_global_device_ids=true | all-gather | bytes 73728 | tf_op jit(solution)/shard_map/all_gather | solution.py:27
  69.1 0.8 gather_fusion
  69.9 1.1 %reshape.694 = bf16[1,2,43,2,32,32]{5,4,3,2,1,0:T(8,128)(2,1)S(1)} reshape(bf16[86,2048]{1,0:T(8,128)(2,1)S(1)} %gather_fusion) | data formatting | bytes 704512 | tf_op jit(solution)/shard_map/gather | solution.py:38
  71.1 0.2 copy_select_fusion
  71.3 0.3 slice_bitcast_fusion.2
  71.6 0.1 fusion.69
  71.7 0.1 add_compare_fusion
  71.8 0.9 fusion.8
  72.8 0.6 copy-done.5
  73.3 1.3 %slice-done.1 = s8[4194304]{0:T(1024)(128)(4,1)S(1)} async-done(((s8[4227072]{0:T(1024)(128)(4,1)}), s8[4194304]{0:T(1024)(128)(4,1)S(1)}, s32[]{:S(2)}) %slice-start.1) | async-done | bytes 4194328
  74.7 1.3 %copy-done.4 = bf16[1,2,43,6,32,32]{5,4,3,2,1,0:T(8,128)(2,1)S(1)} copy-done((bf16[1,2,43,6,32,32]{5,4,3,2,1,0:T(8,128)(2,1)S(1)}, bf16[1,2,43,6,32,32]{5,4,3,2,1,0:T(8,128)(2,1)}, u32[]{:S(2)}) %copy-start.4) | copy-done | bytes 1056792
  75.9 0.8 fusion.23
  76.8 1.5 %fusion.27 = bf16[2,64,32]{1,2,0:T(8,128)(2,1)S(1)} fusion(bf16[2,6,64,32]{2,3,1,0:T(8,128)(2,1)S(1)} %fusion.23, bf16[1,2,43,32,32]{4,3,2,1,0:T(8,128)(2,1)S(1)} %get-tuple-element.15, bf16[1,2,43,32,32]{4,3,2,1,0:T(8,128)(2,1)S(1)} %get-tuple-element.14, bf16[1,2,43,32,32]{4,3,2,1,0:T(8,128)(2,1)S(1)} %fusion.69, ...), kind=kOutput, calls=%fused_computation.41 | convolution fusion | flops 7155712 | bytes 3772428 | tf_op jit(solution)/shard_map/eanij,eanjc->eaic/dot_general | solution.py:64
  78.2 0.2 fusion.26
  78.5 0.6 fusion.73
  79.1 1.4 %multiply_subtract_fusion = (f32[1,2,32,32]{2,3,1,0:T(8,128)S(1)}, f32[1,2,32,32]{2,3,1,0:T(8,128)S(1)}) fusion(f32[1,2,64,32]{2,3,1,0:T(8,128)S(1)} %fusion.26, f32[]{:T(128)} %bitcast.32, f32[]{:T(128)} %bitcast), kind=kLoop, calls=%fused_computation.75 | loop fusion | flops 12288 | bytes 32776 | tf_op jit(solution)/shard_map/sub | solution.py:77
  80.5 0.1 add.226
  80.7 0.1 sub.10
  80.8 19.6 %psum.7 = f32[2,2048]{1,0:T(2,128)} all-reduce(f32[2,2048]{1,0:T(2,128)S(1)} %pad_maximum_fusion.8), channel_id=1, replica_groups=mesh['energy'=4,'atom'=8] {'energy'}, use_global_device_ids=true, to_apply=%region_1.0 | all-reduce | flops 4096 | bytes 32768 | tf_op jit(solution)/shard_map/psum | solution.py:80
  (48 shorter events, 1.1 us)
Async XLA Ops:
  0.0 22.0 %copy-start = (bf16[1,64,2048]{2,1,0:T(8,128)(2,1)S(1)}, bf16[1,64,2048]{2,1,0:T(8,128)(2,1)}, u32[]{:S(2)}) copy-start(bf16[1,64,2048]{2,1,0:T(8,128)(2,1)} %param.10) | copy-start | bytes 786436
  0.0 13.9 %copy-start.1 = (s32[2,384]{1,0:T(2,128)S(1)}, s32[2,384]{1,0:T(2,128)}, u32[]{:S(2)}) copy-start(s32[2,384]{1,0:T(2,128)} %param.14) | copy-start | bytes 9220
  34.7 8.9 %copy-start.3 = (bf16[1,2,43,6,2,32,32]{6,5,4,3,2,1,0:T(8,128)(2,1)S(1)}, bf16[1,2,43,6,2,32,32]{6,5,4,3,2,1,0:T(8,128)(2,1)}, u32[]{:S(2)}) copy-start(bf16[1,2,43,6,2,32,32]{6,5,4,3,2,1,0:T(8,128)(2,1)} %reshape.609) | copy-start | bytes 6340612
  43.6 2.5 %copy-start.6 = (bf16[1,2,2048]{2,1,0:T(2,128)(2,1)S(1)}, bf16[1,2,2048]{2,1,0:T(2,128)(2,1)}, u32[]{:S(2)}) copy-start(bf16[1,2,2048]{2,1,0:T(2,128)(2,1)} %param.9) | copy-start | bytes 24580
  46.5 9.7 %copy-start.2 = (s32[2,64]{1,0:T(2,128)S(1)}, s32[2,64]{1,0:T(2,128)}, u32[]{:S(2)}) copy-start(s32[2,64]{1,0:T(2,128)} %param.11) | copy-start | bytes 1540
  56.0 15.1 %copy-start.8 = (s32[2]{0:T(128)S(1)}, s32[2]{0:T(128)}, u32[]{:S(2)}) copy-start(s32[2]{0:T(128)} %param.12) | copy-start | bytes 28
  69.9 2.8 %slice-start = ((s8[4227072]{0:T(1024)(128)(4,1)}), s8[32768]{0:T(1024)(128)(4,1)S(1)}, s32[]{:S(2)}) async-start(s8[4227072]{0:T(1024)(128)(4,1)} %bitcast.110), calls=%async_computation | async-start | bytes 65536
  71.1 2.2 %copy-start.5 = (bf16[1,2,43,6,32,32]{5,4,3,2,1,0:T(8,128)(2,1)S(1)}, bf16[1,2,43,6,32,32]{5,4,3,2,1,0:T(8,128)(2,1)}, u32[]{:S(2)}) copy-start(bf16[1,2,43,6,32,32]{5,4,3,2,1,0:T(8,128)(2,1)} %get-tuple-element.13) | copy-start | bytes 3170308
  71.3 3.3 %slice-start.1 = ((s8[4227072]{0:T(1024)(128)(4,1)}), s8[4194304]{0:T(1024)(128)(4,1)S(1)}, s32[]{:S(2)}) async-start(s8[4227072]{0:T(1024)(128)(4,1)} %bitcast.110), calls=%async_computation.1 | async-start | bytes 8388608
  71.6 4.3 %copy-start.4 = (bf16[1,2,43,6,32,32]{5,4,3,2,1,0:T(8,128)(2,1)S(1)}, bf16[1,2,43,6,32,32]{5,4,3,2,1,0:T(8,128)(2,1)}, u32[]{:S(2)}) copy-start(bf16[1,2,43,6,32,32]{5,4,3,2,1,0:T(8,128)(2,1)} %get-tuple-element.12) | copy-start | bytes 3170308
  76.8 1.7 %copy-start.7 = (f32[1,2]{1,0:T(1,128)S(1)}, f32[1,2]{1,0:T(1,128)}, u32[]{:S(2)}) copy-start(f32[1,2]{1,0:T(1,128)} %param.15) | copy-start | bytes 28
where the time goes:
time: 101 us; the launch traced here: 100 us
  local copies, waits for them, and re-layouts  51.6 us (51%)
  blocking collectives  30.3 us (30%)
  matrix products  12.9 us (13%)
  other arithmetic  5.4 us (5%)
    gather x11, local copies, waits for them, and re-layouts, take_rows(): jnp.take_along_axis(table, index.reshape(a_dev, -1), axis=1)  22.1 us
    psum x1, blocking collectives, body(): return lax.psum(local_green, 'energy')  19.6 us
    all_gather x1, blocking collectives, body(): window = lax.all_gather(t_mats, 'atom', axis=1, tiled=True)  10.7 us
    dot_general x1, matrix products, body(): jnp.einsum('easkij,eajc->easkic', g_real[:, :, :n1], start_b, preferred_e...  9.49 us
    reshape x2, local copies, waits for them, and re-layouts, real_form(): parts = block.reshape(block.shape[:-1] + (2, L, L))  9.42 us
    squeeze x2, local copies, waits for them, and re-layouts, real_form(): imag_part = parts[..., 1, :, :]  7.6 us
    unnamed x26, local copies, waits for them, and re-layouts  4.99 us
    gather x1, local copies, waits for them, and re-layouts, body(): g_real = real_form(struct_table[:, pairs])  3.39 us

commit v1 on v0

--- a/solution.py
+++ b/solution.py
@@ -77,7 +77,7 @@
     green_real = jnp.sum(w_real * real_rows - w_imag * imag_rows, axis=0)
     green_imag = jnp.sum(w_real * imag_rows + w_imag * real_rows, axis=0)
     local_green = jnp.concatenate([green_real, green_imag], axis=-1)
-    return lax.psum(local_green, "energy")
+    return jnp.sum(lax.all_gather(local_green, "energy"), axis=0)
 
 
 def solution(mesh):

time: 101 us -> 95 us (0.941)
  blocking collectives: 30.3 us -> 24 us
    psum x1 -> x0, blocking collectives: 19.6 us -> none  [body(): return lax.psum(local_green, 'energy')]
    all_gather x0 -> x1, blocking collectives: none -> 13.4 us  [body(): return jnp.sum(lax.all_gather(local_green, 'energy'), axis=0)]
where the time goes in v1:
time: 95 us; the launch traced here: 94.8 us
  local copies, waits for them, and re-layouts  51.6 us (54%)
  blocking collectives  24 us (25%)
  matrix products  12.9 us (14%)
  other arithmetic  6.04 us (6%)
    gather x11, local copies, waits for them, and re-layouts, take_rows(): jnp.take_along_axis(table, index.reshape(a_dev, -1), axis=1)  22.1 us
    all_gather x1, blocking collectives, body(): return jnp.sum(lax.all_gather(local_green, 'energy'), axis=0)  13.4 us
    all_gather x1, blocking collectives, body(): window = lax.all_gather(t_mats, 'atom', axis=1, tiled=True)  10.7 us
    dot_general x1, matrix products, body(): jnp.einsum('easkij,eajc->easkic', g_real[:, :, :n1], start_b, preferred_e...  9.49 us
    reshape x2, local copies, waits for them, and re-layouts, real_form(): parts = block.reshape(block.shape[:-1] + (2, L, L))  9.42 us
    squeeze x2, local copies, waits for them, and re-layouts, real_form(): imag_part = parts[..., 1, :, :]  7.6 us
    unnamed x26, local copies, waits for them, and re-layouts  4.99 us
    gather x1, local copies, waits for them, and re-layouts, body(): g_real = real_form(struct_table[:, pairs])  3.39 us

profile of v1, /device:TPU:0, one launch (start us, length us, event | category | flops | bytes accessed | tf_op | source)
XLA Modules:
  0.0 94.8 jit_solution(12903183545365849367)
XLA Ops:
  0.0 0.8 slice_bitcast_fusion.6
  0.8 0.1 add.203
  0.9 0.1 add.198
  1.0 0.1 reshape.652
  1.1 2.2 %gather_fusion.2 = s32[72]{0:T(128)S(1)} fusion(s32[2,384]{1,0:T(2,128)} %param.14, s32[72]{0:T(128)S(1)} %reshape.652), kind=kCustom, calls=%fused_computation.4 | custom fusion | bytes 1152 | tf_op jit(solution)/shard_map/jit(take_along_axis)/gather | solution.py:22
  3.3 0.1 reshape.655
  3.7 0.1 add.213
  3.9 0.1 add.215
  4.1 9.7 %gather_fusion.4 = s32[516]{0:T(1024)S(1)} fusion(s32[2,384]{1,0:T(2,128)} %param.13, s32[516]{0:T(1024)S(1)} %reshape.686), kind=kCustom, calls=%fused_computation.clone | custom fusion | bytes 8256 | tf_op jit(solution)/shard_map/jit(take_along_axis)/gather | solution.py:22
  13.9 7.5 %gather_fusion.5 = s32[516]{0:T(1024)S(1)} fusion(s32[2,384]{1,0:T(2,128)S(1)} %copy-done.1, s32[516]{0:T(1024)S(1)} %reshape.686), kind=kCustom, calls=%fused_computation.1.clone | custom fusion | bytes 8256 | tf_op jit(solution)/shard_map/jit(take_along_axis)/gather | solution.py:22
  21.6 0.1 reshape.614
  21.7 0.1 reshape.608
  21.8 0.1 reshape.646
  22.0 3.4 %gather_fusion.1 = bf16[516,2048]{1,0:T(8,128)(2,1)S(1)} fusion(bf16[64,2048]{1,0:T(8,128)(2,1)S(1)} %bitcast.110, s32[1024]{0:T(1024)S(1)} %pad_clamp_fusion), kind=kCustom, calls=%fused_computation.3 | custom fusion | bytes 4229136 | tf_op jit(solution)/shard_map/gather | solution.py:40
  25.4 9.3 %reshape.609 = bf16[1,2,43,6,2,32,32]{6,5,4,3,2,1,0:T(8,128)(2,1)} reshape(bf16[516,2048]{1,0:T(8,128)(2,1)S(1)} %gather_fusion.1) | data formatting | bytes 4227072 | tf_op jit(solution)/shard_map/reshape | solution.py:12
  34.7 7.3 %slice_bitcast_fusion = (bf16[1,2,43,6,32,32]{5,4,3,2,1,0:T(8,128)(2,1)}, bf16[1,2,43,6,32,32]{5,4,3,2,1,0:T(8,128)(2,1)}) fusion(bf16[1,2,43,6,2,32,32]{6,5,4,3,2,1,0:T(8,128)(2,1)} %reshape.609), kind=kLoop, calls=%fused_computation.14 | loop fusion | bytes 4227072 | tf_op jit(solution)/shard_map/squeeze | solution.py:14
  42.1 1.5 %copy-done.3 = bf16[1,2,43,6,2,32,32]{6,5,4,3,2,1,0:T(8,128)(2,1)S(1)} copy-done((bf16[1,2,43,6,2,32,32]{6,5,4,3,2,1,0:T(8,128)(2,1)S(1)}, bf16[1,2,43,6,2,32,32]{6,5,4,3,2,1,0:T(8,128)(2,1)}, u32[]{:S(2)}) %copy-start.3) | copy-done | bytes 2113560
  43.6 2.5 %fusion.70 = bf16[1,2,43,6,32,32]{5,4,3,2,1,0:T(8,128)(2,1)} fusion(bf16[1,2,43,6,2,32,32]{6,5,4,3,2,1,0:T(8,128)(2,1)S(1)} %copy-done.3), kind=kLoop, calls=%fused_computation.115 | loop fusion | flops 528384 | bytes 2113536 | tf_op jit(solution)/shard_map/neg | solution.py:15
  46.1 0.1 reshape.616
  46.2 0.1 copy.45
  46.3 0.1 copy.44
  46.4 0.1 convert_bitcast_fusion
  46.5 9.5 %select_reduce_fusion = bf16[2,36,64,32]{2,3,1,0:T(8,128)(2,1)S(1)} fusion(pred[2,36,6]{2,1,0:T(8,128)(4,1)S(1)} %slice_compare_fusion, bf16[1,2,43,6,32,32]{5,4,3,2,1,0:T(8,128)(2,1)} %get-tuple-element.13, bf16[1,2,43,6,32,32]{5,4,3,2,1,0:T(8,128)(2,1)} %get-tuple-element.12, bf16[1,2,43,6,32,32]{5,4,3,2,1,0:T(8,128)(2,1)} %fusion.70, ...), kind=kOutput, calls=%fused_computation.13 | convolution fusion | flops 129024000 | bytes 3473840 | tf_op jit(solution)/shard_map/easkij,eajc->easkic/dot_general | solution.py:44
  56.0 0.1 shift-left_or_fusion
  56.1 0.1 reshape.658
  56.2 2.0 %gather_fusion.3 = s32[86]{0:T(128)S(1)} fusion(s32[2,64]{1,0:T(2,128)S(1)} %copy-done.2, s32[86]{0:T(128)S(1)} %reshape.658), kind=kCustom, calls=%fused_computation.5 | custom fusion | bytes 1376 | tf_op jit(solution)/shard_map/jit(take_along_axis)/gather | solution.py:22
  58.2 0.1 gather.23
  58.3 0.1 reshape.636
  58.4 10.7 %all_gather.9 = bf16[1,16,2048]{2,0,1:T(2,128)(2,1)S(1)} all-gather(bf16[1,2,2048]{2,0,1:T(2,128)(2,1)S(1)} %copy.27), channel_id=1, replica_groups=mesh['energy'=4,'atom'=8] {'atom'}, dimensions={1}, use_global_device_ids=true | all-gather | bytes 73728 | tf_op jit(solution)/shard_map/all_gather | solution.py:27
  69.1 0.8 gather_fusion
  69.9 1.1 %reshape.698 = bf16[1,2,43,2,32,32]{5,4,3,2,1,0:T(8,128)(2,1)S(1)} reshape(bf16[86,2048]{1,0:T(8,128)(2,1)S(1)} %gather_fusion) | data formatting | bytes 704512 | tf_op jit(solution)/shard_map/gather | solution.py:38
  71.1 0.2 copy_select_fusion
  71.3 0.3 slice_bitcast_fusion.2
  71.6 0.1 fusion.69
  71.7 0.1 add_compare_fusion
  71.8 0.9 %fusion.8 = bf16[2,36,64,32]{2,3,1,0:T(8,128)(2,1)S(1)} fusion(bf16[1,2,43,32,32]{4,3,2,1,0:T(8,128)(2,1)S(1)} %get-tuple-element.15, bf16[1,2,43,32,32]{4,3,2,1,0:T(8,128)(2,1)S(1)} %get-tuple-element.14, bf16[1,2,43,32,32]{4,3,2,1,0:T(8,128)(2,1)S(1)} %fusion.69, f32[2,64,32]{1,2,0:T(8,128)S(1)} %get-tuple-element.8, ...), kind=kOutput, calls=%fused_computation.18 | convolution fusion | flops 21676032 | bytes 1134664 | tf_op jit(solution)/shard_map/easij,easjc->easic/dot_general | solution.py:49
  72.8 0.6 copy-done.5
  73.3 1.3 %slice-done.1 = s8[4194304]{0:T(1024)(128)(4,1)S(1)} async-done(((s8[4227072]{0:T(1024)(128)(4,1)}), s8[4194304]{0:T(1024)(128)(4,1)S(1)}, s32[]{:S(2)}) %slice-start.1) | async-done | bytes 4194328
  74.7 1.3 %copy-done.4 = bf16[1,2,43,6,32,32]{5,4,3,2,1,0:T(8,128)(2,1)S(1)} copy-done((bf16[1,2,43,6,32,32]{5,4,3,2,1,0:T(8,128)(2,1)S(1)}, bf16[1,2,43,6,32,32]{5,4,3,2,1,0:T(8,128)(2,1)}, u32[]{:S(2)}) %copy-start.4) | copy-done | bytes 1056792
  75.9 0.8 fusion.23
  76.8 1.5 %fusion.27 = bf16[2,64,32]{1,2,0:T(8,128)(2,1)S(1)} fusion(bf16[2,6,64,32]{2,3,1,0:T(8,128)(2,1)S(1)} %fusion.23, bf16[1,2,43,32,32]{4,3,2,1,0:T(8,128)(2,1)S(1)} %get-tuple-element.15, bf16[1,2,43,32,32]{4,3,2,1,0:T(8,128)(2,1)S(1)} %get-tuple-element.14, bf16[1,2,43,32,32]{4,3,2,1,0:T(8,128)(2,1)S(1)} %fusion.69, ...), kind=kOutput, calls=%fused_computation.41 | convolution fusion | flops 7155712 | bytes 3772428 | tf_op jit(solution)/shard_map/eanij,eanjc->eaic/dot_general | solution.py:64
  78.2 0.2 fusion.26
  78.5 0.6 fusion.73
  79.1 1.4 %multiply_subtract_fusion = (f32[1,2,32,32]{2,3,1,0:T(8,128)S(1)}, f32[1,2,32,32]{2,3,1,0:T(8,128)S(1)}) fusion(f32[1,2,64,32]{2,3,1,0:T(8,128)S(1)} %fusion.26, f32[]{:T(128)} %bitcast.32, f32[]{:T(128)} %bitcast), kind=kLoop, calls=%fused_computation.75 | loop fusion | flops 12288 | bytes 32776 | tf_op jit(solution)/shard_map/sub | solution.py:77
  80.5 0.1 add.224
  80.7 0.1 sub.10
  80.8 13.4 %all-gather.1 = f32[4,2,2048]{2,1,0:T(2,128)S(1)} all-gather(f32[1,2,2048]{2,1,0:T(2,128)S(1)} %maximum_bitcast_fusion.13), channel_id=2, replica_groups=mesh['energy'=4,'atom'=8] {'energy'}, dimensions={0}, use_global_device_ids=true | all-gather | bytes 81920 | tf_op jit(solution)/shard_map/all_gather | solution.py:80
  94.1 0.6 reduce_sum.20
  (49 shorter events, 1.1 us)
Async XLA Ops:
  0.0 22.0 %copy-start = (bf16[1,64,2048]{2,1,0:T(8,128)(2,1)S(1)}, bf16[1,64,2048]{2,1,0:T(8,128)(2,1)}, u32[]{:S(2)}) copy-start(bf16[1,64,2048]{2,1,0:T(8,128)(2,1)} %param.10) | copy-start | bytes 786436
  0.0 13.9 %copy-start.1 = (s32[2,384]{1,0:T(2,128)S(1)}, s32[2,384]{1,0:T(2,128)}, u32[]{:S(2)}) copy-start(s32[2,384]{1,0:T(2,128)} %param.14) | copy-start | bytes 9220
  34.7 8.9 %copy-start.3 = (bf16[1,2,43,6,2,32,32]{6,5,4,3,2,1,0:T(8,128)(2,1)S(1)}, bf16[1,2,43,6,2,32,32]{6,5,4,3,2,1,0:T(8,128)(2,1)}, u32[]{:S(2)}) copy-start(bf16[1,2,43,6,2,32,32]{6,5,4,3,2,1,0:T(8,128)(2,1)} %reshape.609) | copy-start | bytes 6340612
  43.6 2.5 %copy-start.6 = (bf16[1,2,2048]{2,1,0:T(2,128)(2,1)S(1)}, bf16[1,2,2048]{2,1,0:T(2,128)(2,1)}, u32[]{:S(2)}) copy-start(bf16[1,2,2048]{2,1,0:T(2,128)(2,1)} %param.9) | copy-start | bytes 24580
  46.5 9.7 %copy-start.2 = (s32[2,64]{1,0:T(2,128)S(1)}, s32[2,64]{1,0:T(2,128)}, u32[]{:S(2)}) copy-start(s32[2,64]{1,0:T(2,128)} %param.11) | copy-start | bytes 1540
  56.0 15.1 %copy-start.8 = (s32[2]{0:T(128)S(1)}, s32[2]{0:T(128)}, u32[]{:S(2)}) copy-start(s32[2]{0:T(128)} %param.12) | copy-start | bytes 28
  69.9 2.8 %slice-start = ((s8[4227072]{0:T(1024)(128)(4,1)}), s8[32768]{0:T(1024)(128)(4,1)S(1)}, s32[]{:S(2)}) async-start(s8[4227072]{0:T(1024)(128)(4,1)} %bitcast.112), calls=%async_computation | async-start | bytes 65536
  71.1 2.2 %copy-start.5 = (bf16[1,2,43,6,32,32]{5,4,3,2,1,0:T(8,128)(2,1)S(1)}, bf16[1,2,43,6,32,32]{5,4,3,2,1,0:T(8,128)(2,1)}, u32[]{:S(2)}) copy-start(bf16[1,2,43,6,32,32]{5,4,3,2,1,0:T(8,128)(2,1)} %get-tuple-element.13) | copy-start | bytes 3170308
  71.3 3.3 %slice-start.1 = ((s8[4227072]{0:T(1024)(128)(4,1)}), s8[4194304]{0:T(1024)(128)(4,1)S(1)}, s32[]{:S(2)}) async-start(s8[4227072]{0:T(1024)(128)(4,1)} %bitcast.112), calls=%async_computation.1 | async-start | bytes 8388608
  71.6 4.3 %copy-start.4 = (bf16[1,2,43,6,32,32]{5,4,3,2,1,0:T(8,128)(2,1)S(1)}, bf16[1,2,43,6,32,32]{5,4,3,2,1,0:T(8,128)(2,1)}, u32[]{:S(2)}) copy-start(bf16[1,2,43,6,32,32]{5,4,3,2,1,0:T(8,128)(2,1)} %get-tuple-element.12) | copy-start | bytes 3170308
  76.8 1.7 %copy-start.7 = (f32[1,2]{1,0:T(1,128)S(1)}, f32[1,2]{1,0:T(1,128)}, u32[]{:S(2)}) copy-start(f32[1,2]{1,0:T(1,128)} %param.15) | copy-start | bytes 28
